TPU v7x, 256 devices: a whole 4x4x8 slice. The times are simulated.
256 devices in a mesh: ctx: 64 (over y, z, core), tp: 4 (over x).
Axes of the slice: x: 4, y: 4, z: 8, core: 2. Of those that a mesh axis runs over, the one named last changes fastest.
Arguments:
- queries: bfloat16 [32768, 4096], P('ctx', 'tp'), may hold values from -160 to 160
- keys: bfloat16 [32768, 512], P('ctx', 'tp'), may hold values from -5 to 5
- values: bfloat16 [32768, 512], P('ctx', 'tp'), may hold values from -6.5 to 6.5
- evicted: int32 [32768, 4], P('ctx', 'tp'), may hold values 0 or 1
- block_lists: int32 [256, 2], P('ctx'), may hold values from 0 to 6, as said below
- map_query: bfloat16 [4, 128, 64], P('tp'), may hold values from -0.5 to 0.5
- map_key: bfloat16 [4, 128, 64], P('tp'), may hold values from -0.5 to 0.5
- state_gain: float32 [4], P('tp'), may hold values from 0.001953125 to 0.0078125
- out_weight: bfloat16 [4096, 8192], P('tp', 'ctx'), may hold values from -0.09375 to 0.09375
Outputs:
- layer_out: bfloat16 [32768, 8192], P('ctx', 'tp')
Inputs may be any that keep to these rules, and one draw needn't show every extreme that they name: `block_lists`: query block b with local index i = b % (4) lists entry 0 = 4 + i - 1 and entry 1 in 0 to 4 + i - 2, so the two entries differ and lie before the diagonal block.
All inputs are finite; a program needn't handle non-finite values. No bound on the sum of `evicted` on one device may be relied on, other than what follows from the above.
Results may differ from a plain program's by a relative error of at most 0.012.
Values may be sent and summed in bfloat16 or wider, within the bound.
No kernel may reach another device: no remote copies, remote signals or barrier semaphores. Data moves between devices by JAX's collectives and lax.ppermute only.
A program may use at most 128 MiB of HBM per device.

v0:
```python
import jax
import jax.numpy as jnp
from jax import lax
from jax.sharding import Mesh
from jax.sharding import PartitionSpec as P

CTX = ("ctx_0", "ctx_1", "ctx_2")


def passed_along(block, axis, distance):
    devices = range(lax.axis_size(axis))
    route = [(i - distance, i) for i in devices if i - distance in devices]
    return lax.ppermute(block, axis, route)


def neutral_like(shard, identity):
    return jax.tree.map(
        lambda a, e: jnp.broadcast_to(jnp.asarray(e, a.dtype), a.shape), shard, identity
    )


def all_in_one(shard, axis):
    leaves = jax.tree.leaves(shard)
    order = sorted(range(len(leaves)), key=lambda k: -leaves[k].size)
    width = (1, *leaves[order[0]].shape)[-1]
    lines = [
        jnp.pad(leaves[k].reshape(-1), (0, -leaves[k].size % width)).reshape(-1, width)
        for k in order
    ]
    both, at, found = (lax.all_gather(jnp.concatenate(lines), axis), 0, {})
    for k, line in zip(order, lines):
        slab = both[:, at : at + len(line)].reshape(len(both), -1)
        found[k] = slab[:, : leaves[k].size].reshape(-1, *leaves[k].shape)
        at += len(line)
    numbers = iter(range(len(leaves)))
    return jax.tree.map(lambda _: found[next(numbers)], shard)


def carried_in(shard, axes, combine, identity):
    before = start = neutral_like(shard, identity)
    running = shard
    for axis in reversed(axes):
        devices, here = (lax.axis_size(axis), lax.axis_index(axis))
        pieces = all_in_one(
            jax.tree.map(
                lambda part, kind: part.astype(kind), running, (jnp.bfloat16, jnp.bfloat16)
            ),
            axis,
        )
        inside, running = (start, start)
        for k in range(devices):
            passed = k < here
            running = combine(
                running, jax.tree.map(lambda part, own: part[k].astype(own.dtype), pieces, shard)
            )
            inside = jax.tree.map(lambda new, old: jnp.where(passed, new, old), running, inside)
        before = combine(inside, before)
    return before


def feature(inputs, kernel):
    return jax.nn.elu(jnp.dot(inputs, kernel, preferred_element_type=jnp.float32)) + 1.0


def add_pair(earlier, later):
    return (earlier[0] + later[0], earlier[1] + later[1])


def body(queries, keys, values, evicted, block_lists, map_query, map_key, state_gain, out_weight):
    tok_rows = keys.shape[0]
    groups_here = map_key.shape[0]
    head_dim = map_key.shape[1]
    blocks_dev = block_lists.shape[0]
    block_rows = tok_rows // blocks_dev
    group_size = queries.shape[1] // (groups_here * head_dim)
    highest = lax.Precision.HIGHEST
    device = lax.axis_index(CTX)
    width_kv = groups_here * head_dim
    neighbour = passed_along(jnp.concatenate([keys, values], axis=1), CTX, 1)
    left_keys = neighbour[:, :width_kv]
    left_values = neighbour[:, width_kv:]
    group = 0
    key_feats = feature(keys, map_key[group]) * evicted.astype(jnp.float32)
    state_terms = [
        jnp.einsum("tr,th->rh", key_feats, values.astype(jnp.float32), precision=highest)
    ]
    norm_terms = [jnp.sum(key_feats, axis=0)]
    totals = jnp.stack(state_terms)
    counts = jnp.stack(norm_terms)
    packed = jnp.concatenate(
        [totals[0], jnp.pad(counts, ((0, 0), (0, totals.shape[2] - counts.shape[1])))], axis=0
    ).astype(jnp.float32)
    before = jnp.zeros_like(packed)
    running = packed
    for axis in reversed(CTX):
        size, here = (lax.axis_size(axis), lax.axis_index(axis))
        whole = running
        for shift in range(1, size):
            arrived = lax.ppermute(running, axis, [(i, (i + shift) % size) for i in range(size)])
            before = before + jnp.where(shift <= here, arrived, 0.0)
            whole = whole + arrived
        running = whole
    states = before[None, : totals.shape[1]]
    norms = before[None, totals.shape[1], : counts.shape[1]]
    scale = head_dim ** (-0.5)
    offsets = jnp.arange(block_rows, dtype=jnp.int32)
    group = 0
    window_keys = jnp.concatenate([left_keys, keys], axis=0).reshape(
        2 * blocks_dev, block_rows, head_dim
    )
    window_values = jnp.concatenate([left_values, values], axis=0).reshape(
        2 * blocks_dev, block_rows, head_dim
    )
    query_group = queries.reshape(tok_rows, group_size, head_dim)
    query_feats = feature(query_group, map_query[group])
    reads = jnp.einsum("qhr,rd->qhd", query_feats, states[group], precision=highest)
    mass = jnp.einsum("qhr,r->qh", query_feats, norms[group], precision=highest)
    row_pieces = []
    for local in range(blocks_dev):
        chosen = jnp.concatenate(
            [block_lists[local], jnp.full((1,), blocks_dev + local, jnp.int32)]
        )
        key_rows = jnp.take(window_keys, chosen, axis=0).reshape(-1, head_dim)
        value_rows = jnp.take(window_values, chosen, axis=0).reshape(-1, head_dim)
        positions = (
            ((device - 1) * tok_rows + chosen * block_rows)[:, None] + offsets[None, :]
        ).reshape(-1)
        query_pos = device * tok_rows + local * block_rows + offsets
        valid = (positions[None, :] >= 0) & (positions[None, :] <= query_pos[:, None])
        rows_here = slice(local * block_rows, (local + 1) * block_rows)
        query = query_group[rows_here]
        scores = (
            jnp.einsum("qhd,kd->qhk", query, key_rows, preferred_element_type=jnp.float32) * scale
        )
        scores = jnp.where(valid[:, None, :], scores, -jnp.inf)
        top = jnp.max(scores, axis=2)
        weights = jnp.exp(scores - top[:, :, None])
        total = jnp.sum(weights, axis=2)
        probs = weights.astype(jnp.bfloat16)
        numer = jnp.einsum("qhk,kd->qhd", probs, value_rows, preferred_element_type=jnp.float32)
        damping = jnp.exp(-top) * state_gain[group]
        mixed = (numer + damping[:, :, None] * reads[rows_here]) / (
            total + damping * mass[rows_here]
        )[:, :, None]
        row_pieces.append(mixed.reshape(block_rows, group_size * head_dim).astype(jnp.bfloat16))
    group_cols = jnp.concatenate(row_pieces, axis=0)
    n_tp = lax.axis_size("tp")
    swap = [
        (rows * n_tp + group, (rows - group) % n_tp * n_tp + rows)
        for group in range(n_tp)
        for rows in range(n_tp)
    ]
    moved = lax.ppermute(out_weight, ("ctx_0", "tp"), swap)
    gathered = lax.all_gather(moved, CTX, axis=1, tiled=True)
    width = gathered.shape[1] // n_tp
    summed = None
    for shift in range(n_tp):
        if shift == 0:
            rows_in = group_cols
        else:
            rows_in = lax.ppermute(group_cols, "tp", [(i, (i + shift) % n_tp) for i in range(n_tp)])
        term = jnp.dot(
            rows_in,
            gathered[:, shift * width : (shift + 1) * width],
            preferred_element_type=jnp.float32,
        )
        summed = term if summed is None else summed + term
    return summed.astype(jnp.bfloat16)


def solution(mesh):
    finer = Mesh(mesh.devices.reshape(4, 8, 2, mesh.shape["tp"]), ("ctx_0", "ctx_1", "ctx_2", "tp"))
    placed = (
        P(CTX, "tp"),
        P(CTX, "tp"),
        P(CTX, "tp"),
        P(CTX, "tp"),
        P(CTX, None),
        P("tp", None, None),
        P("tp", None, None),
        P("tp"),
        P("tp", CTX),
    )
    return jax.shard_map(body, mesh=finer, in_specs=placed, out_specs=P(CTX, "tp"), check_vma=False)
```

profile of v0, /device:TPU:1, one launch (start us, length us, event | category | flops | bytes accessed | tf_op | source)
XLA Modules:
  0.0 166.2 jit_solution(2092512514743972706)
XLA Ops:
  6.5 1.7 %collective-permute-start.12 = (bf16[1024,128]{1,0:T(8,128)(2,1)}, bf16[1024,128]{1,0:T(8,128)(2,1)S(1)}, u32[]{:S(2)}, u32[]{:S(2)}) collective-permute-start(bf16[1024,128]{1,0:T(8,128)(2,1)} %param.19), channel_id=1, source_target_pairs={{0,0},{64,65},{128,130},{192,195},{1,192},{65,1},{129,66},{193,131... | collective-permute-start | bytes 786440 | tf_op jit(solution)/shard_map/ppermute | solution.py:153
  12.1 3.3 %collective-permute-start.1 = (f32[65,128]{1,0:T(8,128)S(1)}, f32[65,128]{1,0:T(8,128)S(1)}, u32[]{:S(2)}, u32[]{:S(2)}) collective-permute-start(f32[65,128]{1,0:T(8,128)S(1)} %select_maximum_fusion), channel_id=1, source_target_pairs={{0,4},{4,0},{1,5},{5,1},{2,6},{6,2},{3,7},{7,3},{8,12},{12,8},{9,1... | collective-permute-start | bytes 99848 | tf_op jit(solution)/shard_map/ppermute | solution.py:99
  17.9 1.7 %pad_maximum_fusion.1 = bf16[512,256]{1,0:T(8,128)(2,1)} fusion(bf16[512,128]{1,0:T(8,128)(2,1)} %param.13, bf16[512,128]{1,0:T(8,128)(2,1)} %param.12), kind=kLoop, calls=%fused_computation.74 | loop fusion | flops 524288 | bytes 524288 | tf_op jit(solution)/shard_map/concatenate | solution.py:79
  24.5 3.9 %collective-permute-start.8 = (f32[65,128]{1,0:T(8,128)S(1)}, f32[65,128]{1,0:T(8,128)S(1)}, u32[]{:S(2)}, u32[]{:S(2)}) collective-permute-start(f32[65,128]{1,0:T(8,128)S(1)} %fusion.76), channel_id=1, source_target_pairs={{0,56},{8,0},{16,8},{24,16},{32,24},{40,32},{48,40},{56,48},{1,57}... | collective-permute-start | bytes 99848 | tf_op jit(solution)/shard_map/ppermute | solution.py:99
  30.8 4.5 %collective-permute-start.5 = (f32[65,128]{1,0:T(8,128)S(1)}, f32[65,128]{1,0:T(8,128)S(1)}, u32[]{:S(2)}, u32[]{:S(2)}) collective-permute-start(f32[65,128]{1,0:T(8,128)S(1)} %fusion.76), channel_id=1, source_target_pairs={{0,32},{8,40},{16,48},{24,56},{32,0},{40,8},{48,16},{56,24},{1,33}... | collective-permute-start | bytes 99848 | tf_op jit(solution)/shard_map/ppermute | solution.py:99
  35.3 2.2 %collective-permute-start.3 = (f32[65,128]{1,0:T(8,128)S(1)}, f32[65,128]{1,0:T(8,128)S(1)}, u32[]{:S(2)}, u32[]{:S(2)}) collective-permute-start(f32[65,128]{1,0:T(8,128)S(1)} %fusion.76), channel_id=1, source_target_pairs={{0,16},{8,24},{16,32},{24,40},{32,48},{40,56},{48,0},{56,8},{1,17}... | collective-permute-start | bytes 99848 | tf_op jit(solution)/shard_map/ppermute | solution.py:99
  37.4 1.4 collective-permute-start.2
  39.4 4.5 %collective-permute-start = (bf16[512,256]{1,0:T(8,128)(2,1)}, bf16[512,256]{1,0:T(8,128)(2,1)}, u32[]{:S(2)}, u32[]{:S(2)}) collective-permute-start(bf16[512,256]{1,0:T(8,128)(2,1)} %pad_maximum_fusion.1), channel_id=1, source_target_pairs={{0,4},{4,8},{8,12},{12,16},{16,20},{20,24},{24,28},{28,32},{32,36}... | collective-permute-start | bytes 786440 | tf_op jit(solution)/shard_map/ppermute | solution.py:13
  44.0 18.8 %collective-permute-start.11 = (f32[65,128]{1,0:T(8,128)S(1)}, f32[65,128]{1,0:T(8,128)S(1)}, u32[]{:S(2)}, u32[]{:S(2)}) collective-permute-start(f32[65,128]{1,0:T(8,128)S(1)} %add_add_fusion), channel_id=1, source_target_pairs={{0,192},{64,0},{128,64},{192,128},{1,193},{65,1},{129,65},{193,129... | collective-permute-start | bytes 99848 | tf_op jit(solution)/shard_map/ppermute | solution.py:99
  62.8 1.7 %collective-permute-start.10 = (f32[65,128]{1,0:T(8,128)S(1)}, f32[65,128]{1,0:T(8,128)S(1)}, u32[]{:S(2)}, u32[]{:S(2)}) collective-permute-start(f32[65,128]{1,0:T(8,128)S(1)} %add_add_fusion), channel_id=1, source_target_pairs={{0,128},{64,192},{128,0},{192,64},{1,129},{65,193},{129,1},{193,65... | collective-permute-start | bytes 99848 | tf_op jit(solution)/shard_map/ppermute | solution.py:99
  69.8 3.7 %fusion.39 = f32[1,512,8]{0,1,2:T(8,128)S(1)} fusion(f32[512,8,64]{0,2,1:T(8,128)S(1)} %get-tuple-element.49, u8[512,64]{0,1:T(8,128)(4,1)S(1)} %get-tuple-element.48, f32[65,128]{1,0:T(8,128)S(1)} %select_add_fusion), kind=kOutput, calls=%fused_computation.59 | convolution fusion | flops 4980736 | bytes 1098240 | tf_op jit(solution)/shard_map/qhr,r->qh/dot_general | solution.py:117
  74.7 3.2 %fusion.41 = f32[512,8,128]{0,2,1:T(8,128)S(1)} fusion(f32[512,8,64]{0,2,1:T(8,128)S(1)} %get-tuple-element.49, u8[512,64]{0,1:T(8,128)(4,1)} %copy-done.10, f32[65,128]{1,0:T(8,128)} %copy-done.15), kind=kOutput, calls=%fused_computation.60 | convolution fusion | flops 404488192 | bytes 3211264 | tf_op jit(solution)/shard_map/qhr,rd->qhd/dot_general | solution.py:116
  79.0 1.5 gather_fusion.6
  80.4 1.3 gather_fusion.4
  81.8 1.3 gather_fusion.7
  83.8 1.3 gather_fusion.2
  85.1 1.3 gather_fusion.3
  96.1 2.8 %collective-permute-start.14 = (bf16[512,1024]{0,1:T(8,128)(2,1)S(1)}, bf16[512,1024]{0,1:T(8,128)(2,1)}, u32[]{:S(2)}, u32[]{:S(2)}) collective-permute-start(bf16[512,1024]{0,1:T(8,128)(2,1)S(1)} %pad_maximum_fusion), channel_id=1, source_target_pairs={{0,2},{1,3},{2,0},{3,1},{4,6},{5,7},{6,4},{7,5},{8,10},{9,11},{10,... | collective-permute-start | bytes 3145736 | tf_op jit(solution)/shard_map/ppermute | solution.py:161
  98.9 19.9 %collective-permute-done.13 = bf16[512,1024]{0,1:T(8,128)(2,1)} collective-permute-done((bf16[512,1024]{0,1:T(8,128)(2,1)S(1)}, bf16[512,1024]{0,1:T(8,128)(2,1)}, u32[]{:S(2)}, u32[]{:S(2)}) %collective-permute-start.13) | collective-permute-done | bytes 1048608 | tf_op jit(solution)/shard_map/ppermute | solution.py:161
  118.8 20.0 %all-gather.2.cloned.1.call-done = bf16[1024,8192]{1,0:T(8,128)(2,1)} async-done(((bf16[1024,128]{1,0:T(8,128)(2,1)}), bf16[1024,8192]{1,0:T(8,128)(2,1)}) %all-gather.2.cloned.1.call-update) | async-done | bytes 16777232 | tf_op jit(solution)/shard_map/all_gather | solution.py:154
  138.8 4.9 %fusion.4 = f32[512,2048]{1,0:T(8,128)S(1)} fusion(bf16[512,1024]{0,1:T(8,128)(2,1)} %collective-permute-done.13, bf16[1024,8192]{1,0:T(8,128)(2,1)} %all-gather.2.cloned.1.call-done), kind=kOutput, calls=%fused_computation.12 | convolution fusion | flops 2147483648 | bytes 9437184 | tf_op jit(solution)/shard_map/dot_general | solution.py:162
  143.7 4.9 %fusion.2 = f32[512,2048]{1,0:T(8,128)S(1)} fusion(bf16[512,1024]{0,1:T(8,128)(2,1)} %collective-permute-done.14, bf16[1024,8192]{1,0:T(8,128)(2,1)} %all-gather.2.cloned.1.call-done), kind=kOutput, calls=%fused_computation.10 | convolution fusion | flops 2147483648 | bytes 9437184 | tf_op jit(solution)/shard_map/dot_general | solution.py:162
  148.6 4.6 %fusion.6 = f32[512,2048]{1,0:T(8,128)S(1)} fusion(bf16[1024,8192]{1,0:T(8,128)(2,1)} %all-gather.2.cloned.1.call-done, bf16[128,1024]{0,1:T(8,128)(2,1)S(1)} %bitcast.129, bf16[128,1024]{0,1:T(8,128)(2,1)S(1)} %bitcast.127, bf16[128,1024]{0,1:T(8,128)(2,1)S(1)} %bitcast.125, bf16[128,1024]{0,1:T(8,128)(2,1)S(1)} %bitcast.131), kind=kOutput, calls=%fused_computation.14 | convolution fusion | flops 2151677952 | bytes 9437184 | tf_op jit(solution)/shard_map/dot_general | solution.py:162
  153.2 6.2 %add_convert_fusion = bf16[512,2048]{1,0:T(8,128)(2,1)} fusion(f32[512,2048]{1,0:T(8,128)S(1)} %fusion.2, f32[512,2048]{1,0:T(8,128)S(1)} %fusion.6, f32[512,2048]{1,0:T(8,128)S(1)} %fusion.4, bf16[512,1024]{0,1:T(8,128)(2,1)S(1)} %collective-permute-done.15, bf16[1024,8192]{1,0:T(8,128)(2,1)} %all-gather.2.cloned.1.call-done), kind=kOutput, calls=%fused_computation.16 | convolution fusion | flops 2151677952 | bytes 19922944 | tf_op jit(solution)/shard_map/dot_general | solution.py:162
  (126 shorter events, 31.1 us)
Async XLA Ops:
  6.5 16.8 %copy-start = (bf16[1,128,64]{1,2,0:T(8,128)(2,1)S(1)}, bf16[1,128,64]{1,2,0:T(8,128)(2,1)}, u32[]{:S(2)}) copy-start(bf16[1,128,64]{1,2,0:T(8,128)(2,1)} %param.16) | copy-start | bytes 49156
  6.5 16.8 %copy-start.1 = (bf16[512,1024]{1,0:T(8,128)(2,1)S(1)}, bf16[512,1024]{1,0:T(8,128)(2,1)}, u32[]{:S(2)}) copy-start(bf16[512,1024]{1,0:T(8,128)(2,1)} %param.11) | copy-start | bytes 3145732
  6.5 132.2 %all-gather.2.cloned.1.call-start = ((), (), s32[]{:S(2)}) async-start(), calls=%async_computation | async-start | bytes 17039360 | tf_op jit(solution)/shard_map/all_gather | solution.py:154
  6.5 1.7 %collective-permute-start.12 = (bf16[1024,128]{1,0:T(8,128)(2,1)}, bf16[1024,128]{1,0:T(8,128)(2,1)S(1)}, u32[]{:S(2)}, u32[]{:S(2)}) collective-permute-start(bf16[1024,128]{1,0:T(8,128)(2,1)} %param.19), channel_id=1, source_target_pairs={{0,0},{64,65},{128,130},{192,195},{1,192},{65,1},{129,66},{193,131... | collective-permute-start | bytes 786440 | tf_op jit(solution)/shard_map/ppermute | solution.py:153
  12.1 12.4 %collective-permute-start.1 = (f32[65,128]{1,0:T(8,128)S(1)}, f32[65,128]{1,0:T(8,128)S(1)}, u32[]{:S(2)}, u32[]{:S(2)}) collective-permute-start(f32[65,128]{1,0:T(8,128)S(1)} %select_maximum_fusion), channel_id=1, source_target_pairs={{0,4},{4,0},{1,5},{5,1},{2,6},{6,2},{3,7},{7,3},{8,12},{12,8},{9,1... | collective-permute-start | bytes 99848 | tf_op jit(solution)/shard_map/ppermute | solution.py:99
  23.9 49.6 %copy-start.10 = (u8[512,64]{0,1:T(8,128)(4,1)}, u8[512,64]{0,1:T(8,128)(4,1)S(1)}, u32[]{:S(2)}) copy-start(u8[512,64]{0,1:T(8,128)(4,1)S(1)} %get-tuple-element.48) | copy-start | bytes 98308
  24.5 10.7 %collective-permute-start.8 = (f32[65,128]{1,0:T(8,128)S(1)}, f32[65,128]{1,0:T(8,128)S(1)}, u32[]{:S(2)}, u32[]{:S(2)}) collective-permute-start(f32[65,128]{1,0:T(8,128)S(1)} %fusion.76), channel_id=1, source_target_pairs={{0,56},{8,0},{16,8},{24,16},{32,24},{40,32},{48,40},{56,48},{1,57}... | collective-permute-start | bytes 99848 | tf_op jit(solution)/shard_map/ppermute | solution.py:99
  28.5 8.9 %collective-permute-start.7 = (f32[65,128]{1,0:T(8,128)S(1)}, f32[65,128]{1,0:T(8,128)S(1)}, u32[]{:S(2)}, u32[]{:S(2)}) collective-permute-start(f32[65,128]{1,0:T(8,128)S(1)} %fusion.76), channel_id=1, source_target_pairs={{0,48},{8,56},{16,0},{24,8},{32,16},{40,24},{48,32},{56,40},{1,49}... | collective-permute-start | bytes 99848 | tf_op jit(solution)/shard_map/ppermute | solution.py:99
  30.3 9.1 %collective-permute-start.6 = (f32[65,128]{1,0:T(8,128)S(1)}, f32[65,128]{1,0:T(8,128)S(1)}, u32[]{:S(2)}, u32[]{:S(2)}) collective-permute-start(f32[65,128]{1,0:T(8,128)S(1)} %fusion.76), channel_id=1, source_target_pairs={{0,40},{8,48},{16,56},{24,0},{32,8},{40,16},{48,24},{56,32},{1,41}... | collective-permute-start | bytes 99848 | tf_op jit(solution)/shard_map/ppermute | solution.py:99
  30.8 13.2 %collective-permute-start.5 = (f32[65,128]{1,0:T(8,128)S(1)}, f32[65,128]{1,0:T(8,128)S(1)}, u32[]{:S(2)}, u32[]{:S(2)}) collective-permute-start(f32[65,128]{1,0:T(8,128)S(1)} %fusion.76), channel_id=1, source_target_pairs={{0,32},{8,40},{16,48},{24,56},{32,0},{40,8},{48,16},{56,24},{1,33}... | collective-permute-start | bytes 99848 | tf_op jit(solution)/shard_map/ppermute | solution.py:99
  35.3 8.7 %collective-permute-start.4 = (f32[65,128]{1,0:T(8,128)S(1)}, f32[65,128]{1,0:T(8,128)S(1)}, u32[]{:S(2)}, u32[]{:S(2)}) collective-permute-start(f32[65,128]{1,0:T(8,128)S(1)} %fusion.76), channel_id=1, source_target_pairs={{0,24},{8,32},{16,40},{24,48},{32,56},{40,0},{48,8},{56,16},{1,25}... | collective-permute-start | bytes 99848 | tf_op jit(solution)/shard_map/ppermute | solution.py:99
  35.3 8.7 %collective-permute-start.3 = (f32[65,128]{1,0:T(8,128)S(1)}, f32[65,128]{1,0:T(8,128)S(1)}, u32[]{:S(2)}, u32[]{:S(2)}) collective-permute-start(f32[65,128]{1,0:T(8,128)S(1)} %fusion.76), channel_id=1, source_target_pairs={{0,16},{8,24},{16,32},{24,40},{32,48},{40,56},{48,0},{56,8},{1,17}... | collective-permute-start | bytes 99848 | tf_op jit(solution)/shard_map/ppermute | solution.py:99
  37.4 6.6 %collective-permute-start.2 = (f32[65,128]{1,0:T(8,128)S(1)}, f32[65,128]{1,0:T(8,128)S(1)}, u32[]{:S(2)}, u32[]{:S(2)}) collective-permute-start(f32[65,128]{1,0:T(8,128)S(1)} %fusion.76), channel_id=1, source_target_pairs={{0,8},{8,16},{16,24},{24,32},{32,40},{40,48},{48,56},{56,0},{1,9},... | collective-permute-start | bytes 99848 | tf_op jit(solution)/shard_map/ppermute | solution.py:99
  39.4 38.5 %collective-permute-start = (bf16[512,256]{1,0:T(8,128)(2,1)}, bf16[512,256]{1,0:T(8,128)(2,1)}, u32[]{:S(2)}, u32[]{:S(2)}) collective-permute-start(bf16[512,256]{1,0:T(8,128)(2,1)} %pad_maximum_fusion.1), channel_id=1, source_target_pairs={{0,4},{4,8},{8,12},{12,16},{16,20},{20,24},{24,28},{28,32},{32,36}... | collective-permute-start | bytes 786440 | tf_op jit(solution)/shard_map/ppermute | solution.py:13
  44.0 24.5 %collective-permute-start.11 = (f32[65,128]{1,0:T(8,128)S(1)}, f32[65,128]{1,0:T(8,128)S(1)}, u32[]{:S(2)}, u32[]{:S(2)}) collective-permute-start(f32[65,128]{1,0:T(8,128)S(1)} %add_add_fusion), channel_id=1, source_target_pairs={{0,192},{64,0},{128,64},{192,128},{1,193},{65,1},{129,65},{193,129... | collective-permute-start | bytes 99848 | tf_op jit(solution)/shard_map/ppermute | solution.py:99
  62.8 5.7 %collective-permute-start.10 = (f32[65,128]{1,0:T(8,128)S(1)}, f32[65,128]{1,0:T(8,128)S(1)}, u32[]{:S(2)}, u32[]{:S(2)}) collective-permute-start(f32[65,128]{1,0:T(8,128)S(1)} %add_add_fusion), channel_id=1, source_target_pairs={{0,128},{64,192},{128,0},{192,64},{1,129},{65,193},{129,1},{193,65... | collective-permute-start | bytes 99848 | tf_op jit(solution)/shard_map/ppermute | solution.py:99
  64.5 4.6 %collective-permute-start.9 = (f32[65,128]{1,0:T(8,128)S(1)}, f32[65,128]{1,0:T(8,128)S(1)}, u32[]{:S(2)}, u32[]{:S(2)}) collective-permute-start(f32[65,128]{1,0:T(8,128)S(1)} %add_add_fusion), channel_id=1, source_target_pairs={{0,64},{64,128},{128,192},{192,0},{1,65},{65,129},{129,193},{193,1... | collective-permute-start | bytes 99848 | tf_op jit(solution)/shard_map/ppermute | solution.py:99
  74.7 4.2 %copy-start.5 = (bf16[512,128]{1,0:T(8,128)(2,1)S(1)}, bf16[512,128]{1,0:T(8,128)(2,1)}, u32[]{:S(2)}) copy-start(bf16[512,128]{1,0:T(8,128)(2,1)} %param.12) | copy-start | bytes 393220
  74.7 7.0 %copy-start.6 = (bf16[512,128]{1,0:T(8,128)(2,1)S(1)}, bf16[512,128]{1,0:T(8,128)(2,1)}, u32[]{:S(2)}) copy-start(bf16[512,128]{1,0:T(8,128)(2,1)} %param.13) | copy-start | bytes 393220
  78.9 9.9 %copy-start.4 = (bf16[128,1024]{0,1:T(8,128)(2,1)S(1)}, bf16[128,1024]{0,1:T(8,128)(2,1)}, u32[]{:S(2)}) copy-start(bf16[128,1024]{0,1:T(8,128)(2,1)} %copy.56) | copy-start | bytes 786436
  88.9 1.6 copy-start.3
  94.9 23.9 %collective-permute-start.13 = (bf16[512,1024]{0,1:T(8,128)(2,1)S(1)}, bf16[512,1024]{0,1:T(8,128)(2,1)}, u32[]{:S(2)}, u32[]{:S(2)}) collective-permute-start(bf16[512,1024]{0,1:T(8,128)(2,1)S(1)} %pad_maximum_fusion), channel_id=1, source_target_pairs={{0,1},{1,2},{2,3},{3,0},{4,5},{5,6},{6,7},{7,4},{8,9},{9,10},{10,1... | collective-permute-start | bytes 3145736 | tf_op jit(solution)/shard_map/ppermute | solution.py:161
  96.1 47.6 %collective-permute-start.14 = (bf16[512,1024]{0,1:T(8,128)(2,1)S(1)}, bf16[512,1024]{0,1:T(8,128)(2,1)}, u32[]{:S(2)}, u32[]{:S(2)}) collective-permute-start(bf16[512,1024]{0,1:T(8,128)(2,1)S(1)} %pad_maximum_fusion), channel_id=1, source_target_pairs={{0,2},{1,3},{2,0},{3,1},{4,6},{5,7},{6,4},{7,5},{8,10},{9,11},{10,... | collective-permute-start | bytes 3145736 | tf_op jit(solution)/shard_map/ppermute | solution.py:161
  98.9 54.3 %collective-permute-start.15 = (bf16[512,1024]{0,1:T(8,128)(2,1)S(1)}, bf16[512,1024]{0,1:T(8,128)(2,1)S(1)}, u32[]{:S(2)}, u32[]{:S(2)}) collective-permute-start(bf16[512,1024]{0,1:T(8,128)(2,1)S(1)} %pad_maximum_fusion), channel_id=1, source_target_pairs={{0,3},{1,0},{2,1},{3,2},{4,7},{5,4},{6,5},{7,6},{8,11},{9,8},{10,9... | collective-permute-start | bytes 3145736 | tf_op jit(solution)/shard_map/ppermute | solution.py:161
  (13 other events, 13.4 us)
Sparse Core Ops, SparseCore 0:
  9.9 128.8 all-gather.1
where the time goes:
time: 167 us; the launch traced here: 166 us
  starting transfers between devices  47.7 us (29%)
  waiting for transfers between devices  40.6 us (24%)
  matrix products  34.3 us (21%)
  local copies, waits for them, and re-layouts  16.7 us (10%)
  between operations  14.6 us (9%)
  other arithmetic  12.4 us (7%)
    ppermute x11, starting transfers between devices, body(): lax.ppermute(running, axis, [(i, (i + shift) % size) for i in range(size)])  37.4 us
    dot_general x4, matrix products, body(): jnp.dot(rows_in, gathered[:, shift * width:(shift + 1) * width], preferre...  20.5 us
    all_gather x1, waiting for transfers between devices, body(): gathered = lax.all_gather(moved, CTX, axis=1, tiled=True)  20 us
    ppermute x3, waiting for transfers between devices, body(): lax.ppermute(group_cols, 'tp', [(i, (i + shift) % n_tp) for i in range(n_...  19.9 us
    gather x4, local copies, waits for them, and re-layouts, body(): key_rows = jnp.take(window_keys, chosen, axis=0).reshape(-1, head_dim)  4.78 us
    unnamed x44, local copies, waits for them, and re-layouts  4.56 us
    ppermute x1, starting transfers between devices, passed_along(): return lax.ppermute(block, axis, route)  4.54 us
    gather x4, local copies, waits for them, and re-layouts, body(): value_rows = jnp.take(window_values, chosen, axis=0).reshape(-1, head_dim)  4.01 us
  transfers between devices with their start and end apart: 17, of which 3 were waited for; matrix products, arithmetic and copies ran while one was open for 33% of the time, Pallas kernels for 0%

commit v1 on v0

--- a/solution.py
+++ b/solution.py
@@ -5,6 +5,13 @@
 from jax.sharding import PartitionSpec as P
 
 CTX = ("ctx_0", "ctx_1", "ctx_2")
+
+
+def shapes_note(sample, in_dim):
+    arr_out = tuple((sample for _ in range(lax.axis_size(CTX))))
+    piece_now = jnp.stack(arr_out, axis=0)
+    carry_out = lax.all_to_all(piece_now, CTX, 0, 0)
+    return jnp.concatenate(carry_out, axis=in_dim)
 
 
 def passed_along(block, axis, distance):
@@ -151,7 +158,7 @@
         for rows in range(n_tp)
     ]
     moved = lax.ppermute(out_weight, ("ctx_0", "tp"), swap)
-    gathered = lax.all_gather(moved, CTX, axis=1, tiled=True)
+    gathered = shapes_note(moved, 1)
     width = gathered.shape[1] // n_tp
     summed = None
     for shift in range(n_tp):

time: 167 us -> 504 us (3.02)
  waiting for transfers between devices: 40.6 us -> 377 us
  between operations: 14.6 us -> 1.21 us
  starting transfers between devices: 47.7 us -> 60 us
    ppermute x11, waiting for transfers between devices: 0.67 us -> 343 us  [body(): lax.ppermute(running, axis, [(i, (i + shift) % size) for i in range(size)])]
    all_to_all x0 -> x1, starting transfers between devices: none -> 28.1 us  [shapes_note(): carry_out = lax.all_to_all(piece_now, CTX, 0, 0)]
    all_gather x1 -> x0, waiting for transfers between devices: 20 us -> none  [body(): gathered = lax.all_gather(moved, CTX, axis=1, tiled=True)]
    ppermute x11, starting transfers between devices: 37.4 us -> 19.9 us  [body(): lax.ppermute(running, axis, [(i, (i + shift) % size) for i in range(size)])]
    ppermute x3, waiting for transfers between devices: 19.9 us -> 34.3 us  [body(): lax.ppermute(group_cols, 'tp', [(i, (i + shift) % n_tp) for i in range(n_...]
    another operation x0 -> x1, local copies, waits for them, and re-layouts: none -> 6.09 us  [shapes_note(): piece_now = jnp.stack(arr_out, axis=0)]
  transfers between devices with their start and end apart: 17 -> 17, of which waited for: 3 -> 5; matrix products, arithmetic and copies ran while one was open for 33% -> 10% of each run, Pallas kernels for 0% -> 0%
where the time goes in v1:
time: 504 us; the launch traced here: 503 us
  waiting for transfers between devices  377 us (75%)
  starting transfers between devices  60 us (12%)
  matrix products  32.9 us (7%)
  local copies, waits for them, and re-layouts  20.5 us (4%)
  other arithmetic  11.3 us (2%)
    ppermute x11, waiting for transfers between devices, body(): lax.ppermute(running, axis, [(i, (i + shift) % size) for i in range(size)])  343 us
    ppermute x3, waiting for transfers between devices, body(): lax.ppermute(group_cols, 'tp', [(i, (i + shift) % n_tp) for i in range(n_...  34.3 us
    all_to_all x1, starting transfers between devices, shapes_note(): carry_out = lax.all_to_all(piece_now, CTX, 0, 0)  28.1 us
    dot_general x4, matrix products, body(): jnp.dot(rows_in, gathered[:, shift * width:(shift + 1) * width], preferre...  20.5 us
    ppermute x11, starting transfers between devices, body(): lax.ppermute(running, axis, [(i, (i + shift) % size) for i in range(size)])  19.9 us
  transfers between devices with their start and end apart: 17, of which 5 were waited for; matrix products, arithmetic and copies ran while one was open for 10% of the time, Pallas kernels for 0%

profile of v1, /device:TPU:1, one launch (start us, length us, event | category | flops | bytes accessed | tf_op | source)
XLA Modules:
  0.0 503.1 jit_solution(16749012649177767324)
XLA Ops:
  0.0 1.7 collective-permute-start.12
  1.9 6.1 %stack.5 = bf16[64,1024,128]{1,2,0:T(8,128)(2,1)} broadcast(bf16[1024,128]{0,1:T(8,128)(2,1)S(1)} %copy.36), dimensions={1,2} | broadcast | bytes 17039360 | tf_op jit(solution)/shard_map/stack | solution.py:12
  8.0 28.1 %all-to-all-start = ((bf16[64,1024,128]{1,2,0:T(8,128)(2,1)}), bf16[64,1024,128]{1,2,0:T(8,128)(2,1)}, u32[]{:S(2)}, u32[]{:S(2)}) async-start(bf16[64,1024,128]{1,2,0:T(8,128)(2,1)} %stack.5), calls=%async_computation | async-start | bytes 33554432 | tf_op jit(solution)/shard_map/all_to_all | solution.py:13
  46.7 2.1 collective-permute-start.3
  48.8 2.4 collective-permute-start.4
  51.2 2.1 collective-permute-start.5
  53.3 2.4 collective-permute-start.6
  55.7 340.1 %collective-permute-done.2 = f32[65,128]{1,0:T(8,128)S(1)} collective-permute-done((f32[65,128]{1,0:T(8,128)S(1)}, f32[65,128]{1,0:T(8,128)S(1)}, u32[]{:S(2)}, u32[]{:S(2)}) %collective-permute-start.2) | collective-permute-done | bytes 33312 | tf_op jit(solution)/shard_map/ppermute | solution.py:106
  395.8 2.7 collective-permute-start.7
  398.5 2.3 collective-permute-done.3
  400.8 1.9 collective-permute-start.8
  403.0 4.8 collective-permute-start
  407.9 3.1 collective-permute-start.10
  417.8 4.5 fusion.39
  423.5 3.1 fusion.41
  442.7 1.6 collective-permute-start.14
  444.4 2.1 collective-permute-start.13
  446.4 1.7 collective-permute-start.15
  448.2 18.1 %collective-permute-done.14 = bf16[512,1024]{0,1:T(8,128)(2,1)} collective-permute-done((bf16[512,1024]{0,1:T(8,128)(2,1)S(1)}, bf16[512,1024]{0,1:T(8,128)(2,1)}, u32[]{:S(2)}, u32[]{:S(2)}) %collective-permute-start.14) | collective-permute-done | bytes 1048608 | tf_op jit(solution)/shard_map/ppermute | solution.py:168
  466.2 4.9 fusion.2
  471.1 4.6 fusion.6
  475.7 16.3 %collective-permute-done.13 = bf16[512,1024]{0,1:T(8,128)(2,1)} collective-permute-done((bf16[512,1024]{0,1:T(8,128)(2,1)S(1)}, bf16[512,1024]{0,1:T(8,128)(2,1)}, u32[]{:S(2)}, u32[]{:S(2)}) %collective-permute-start.13) | collective-permute-done | bytes 1048608 | tf_op jit(solution)/shard_map/ppermute | solution.py:168
  492.0 4.9 fusion.4
  496.9 6.2 %add_convert_fusion = bf16[512,2048]{1,0:T(8,128)(2,1)} fusion(f32[512,2048]{1,0:T(8,128)S(1)} %fusion.2, f32[512,2048]{1,0:T(8,128)S(1)} %fusion.6, f32[512,2048]{1,0:T(8,128)S(1)} %fusion.4, bf16[512,1024]{0,1:T(8,128)(2,1)S(1)} %collective-permute-done.15, bf16[1024,8192]{0,1:T(8,128)(2,1)} %bitcast.45), kind=kOutput, calls=%fused_computation.16 | convolution fusion | flops 2151677952 | bytes 19922944 | tf_op jit(solution)/shard_map/dot_general | solution.py:169
  (135 shorter events, 34.2 us)
Async XLA Ops:
  0.0 43.6 %copy-start = (bf16[1,128,64]{1,2,0:T(8,128)(2,1)S(1)}, bf16[1,128,64]{1,2,0:T(8,128)(2,1)}, u32[]{:S(2)}) copy-start(bf16[1,128,64]{1,2,0:T(8,128)(2,1)} %param.16) | copy-start | bytes 49156
  0.0 1.7 collective-permute-start.12
  8.0 28.2 %copy-start.22 = (s32[512,1]{0,1:T(1,128)S(1)}, s32[512,1]{0,1:T(1,128)}, u32[]{:S(2)}) copy-start(s32[512,1]{0,1:T(1,128)} %param.14) | copy-start | bytes 6148
  8.0 28.2 %copy-start.6 = (bf16[512,128]{1,0:T(8,128)(2,1)S(1)}, bf16[512,128]{1,0:T(8,128)(2,1)}, u32[]{:S(2)}) copy-start(bf16[512,128]{1,0:T(8,128)(2,1)} %param.12) | copy-start | bytes 393220
  8.0 28.2 %copy-start.23 = (bf16[1,128,64]{1,2,0:T(8,128)(2,1)S(1)}, bf16[1,128,64]{1,2,0:T(8,128)(2,1)}, u32[]{:S(2)}) copy-start(bf16[1,128,64]{1,2,0:T(8,128)(2,1)} %param.17) | copy-start | bytes 49156
  8.0 28.5 %copy-start.7 = (bf16[512,128]{1,0:T(8,128)(2,1)S(1)}, bf16[512,128]{1,0:T(8,128)(2,1)}, u32[]{:S(2)}) copy-start(bf16[512,128]{1,0:T(8,128)(2,1)} %param.13) | copy-start | bytes 393220
  8.0 29.4 %copy-start.17 = (s32[4,2]{0,1:T(2,128)S(1)}, s32[4,2]{0,1:T(2,128)}, u32[]{:S(2)}) copy-start(s32[4,2]{0,1:T(2,128)} %param.15) | copy-start | bytes 100
  8.0 458.2 %all-to-all-start = ((bf16[64,1024,128]{1,2,0:T(8,128)(2,1)}), bf16[64,1024,128]{1,2,0:T(8,128)(2,1)}, u32[]{:S(2)}, u32[]{:S(2)}) async-start(bf16[64,1024,128]{1,2,0:T(8,128)(2,1)} %stack.5), calls=%async_computation | async-start | bytes 33554432 | tf_op jit(solution)/shard_map/all_to_all | solution.py:13
  36.8 8.6 %collective-permute-start.1 = (f32[65,128]{1,0:T(8,128)S(1)}, f32[65,128]{1,0:T(8,128)S(1)}, u32[]{:S(2)}, u32[]{:S(2)}) collective-permute-start(f32[65,128]{1,0:T(8,128)S(1)} %select_maximum_fusion), channel_id=1, source_target_pairs={{0,4},{4,0},{1,5},{5,1},{2,6},{6,2},{3,7},{7,3},{8,12},{12,8},{9,1... | collective-permute-start | bytes 99848 | tf_op jit(solution)/shard_map/ppermute | solution.py:106
  45.4 370.1 %copy-start.15 = (f32[65,128]{1,0:T(8,128)}, f32[65,128]{1,0:T(8,128)S(1)}, u32[]{:S(2)}) copy-start(f32[65,128]{1,0:T(8,128)S(1)} %collective-permute-done.1) | copy-start | bytes 99844
  45.4 350.4 %collective-permute-start.2 = (f32[65,128]{1,0:T(8,128)S(1)}, f32[65,128]{1,0:T(8,128)S(1)}, u32[]{:S(2)}, u32[]{:S(2)}) collective-permute-start(f32[65,128]{1,0:T(8,128)S(1)} %fusion.76), channel_id=1, source_target_pairs={{0,8},{8,16},{16,24},{24,32},{32,40},{40,48},{48,56},{56,0},{1,9},... | collective-permute-start | bytes 99848 | tf_op jit(solution)/shard_map/ppermute | solution.py:106
  46.7 354.1 %collective-permute-start.3 = (f32[65,128]{1,0:T(8,128)S(1)}, f32[65,128]{1,0:T(8,128)S(1)}, u32[]{:S(2)}, u32[]{:S(2)}) collective-permute-start(f32[65,128]{1,0:T(8,128)S(1)} %fusion.76), channel_id=1, source_target_pairs={{0,16},{8,24},{16,32},{24,40},{32,48},{40,56},{48,0},{56,8},{1,17}... | collective-permute-start | bytes 99848 | tf_op jit(solution)/shard_map/ppermute | solution.py:106
  48.8 354.2 %collective-permute-start.4 = (f32[65,128]{1,0:T(8,128)S(1)}, f32[65,128]{1,0:T(8,128)S(1)}, u32[]{:S(2)}, u32[]{:S(2)}) collective-permute-start(f32[65,128]{1,0:T(8,128)S(1)} %fusion.76), channel_id=1, source_target_pairs={{0,24},{8,32},{16,40},{24,48},{32,56},{40,0},{48,8},{56,16},{1,25}... | collective-permute-start | bytes 99848 | tf_op jit(solution)/shard_map/ppermute | solution.py:106
  51.2 356.6 %collective-permute-start.5 = (f32[65,128]{1,0:T(8,128)S(1)}, f32[65,128]{1,0:T(8,128)S(1)}, u32[]{:S(2)}, u32[]{:S(2)}) collective-permute-start(f32[65,128]{1,0:T(8,128)S(1)} %fusion.76), channel_id=1, source_target_pairs={{0,32},{8,40},{16,48},{24,56},{32,0},{40,8},{48,16},{56,24},{1,33}... | collective-permute-start | bytes 99848 | tf_op jit(solution)/shard_map/ppermute | solution.py:106
  53.3 354.5 %collective-permute-start.6 = (f32[65,128]{1,0:T(8,128)S(1)}, f32[65,128]{1,0:T(8,128)S(1)}, u32[]{:S(2)}, u32[]{:S(2)}) collective-permute-start(f32[65,128]{1,0:T(8,128)S(1)} %fusion.76), channel_id=1, source_target_pairs={{0,40},{8,48},{16,56},{24,0},{32,8},{40,16},{48,24},{56,32},{1,41}... | collective-permute-start | bytes 99848 | tf_op jit(solution)/shard_map/ppermute | solution.py:106
  395.8 12.0 %collective-permute-start.7 = (f32[65,128]{1,0:T(8,128)S(1)}, f32[65,128]{1,0:T(8,128)S(1)}, u32[]{:S(2)}, u32[]{:S(2)}) collective-permute-start(f32[65,128]{1,0:T(8,128)S(1)} %fusion.76), channel_id=1, source_target_pairs={{0,48},{8,56},{16,0},{24,8},{32,16},{40,24},{48,32},{56,40},{1,49}... | collective-permute-start | bytes 99848 | tf_op jit(solution)/shard_map/ppermute | solution.py:106
  400.8 7.0 %collective-permute-start.8 = (f32[65,128]{1,0:T(8,128)S(1)}, f32[65,128]{1,0:T(8,128)S(1)}, u32[]{:S(2)}, u32[]{:S(2)}) collective-permute-start(f32[65,128]{1,0:T(8,128)S(1)} %fusion.76), channel_id=1, source_target_pairs={{0,56},{8,0},{16,8},{24,16},{32,24},{40,32},{48,40},{56,48},{1,57}... | collective-permute-start | bytes 99848 | tf_op jit(solution)/shard_map/ppermute | solution.py:106
  403.0 23.7 %collective-permute-start = (bf16[512,256]{1,0:T(8,128)(2,1)}, bf16[512,256]{1,0:T(8,128)(2,1)}, u32[]{:S(2)}, u32[]{:S(2)}) collective-permute-start(bf16[512,256]{1,0:T(8,128)(2,1)} %pad_maximum_fusion.1), channel_id=1, source_target_pairs={{0,4},{4,8},{8,12},{12,16},{16,20},{20,24},{24,28},{28,32},{32,36}... | collective-permute-start | bytes 786440 | tf_op jit(solution)/shard_map/ppermute | solution.py:20
  407.9 8.5 %collective-permute-start.10 = (f32[65,128]{1,0:T(8,128)S(1)}, f32[65,128]{1,0:T(8,128)S(1)}, u32[]{:S(2)}, u32[]{:S(2)}) collective-permute-start(f32[65,128]{1,0:T(8,128)S(1)} %add_add_fusion), channel_id=1, source_target_pairs={{0,128},{64,192},{128,0},{192,64},{1,129},{65,193},{129,1},{193,65... | collective-permute-start | bytes 99848 | tf_op jit(solution)/shard_map/ppermute | solution.py:106
  410.9 5.4 %collective-permute-start.11 = (f32[65,128]{1,0:T(8,128)S(1)}, f32[65,128]{1,0:T(8,128)S(1)}, u32[]{:S(2)}, u32[]{:S(2)}) collective-permute-start(f32[65,128]{1,0:T(8,128)S(1)} %add_add_fusion), channel_id=1, source_target_pairs={{0,192},{64,0},{128,64},{192,128},{1,193},{65,1},{129,65},{193,129... | collective-permute-start | bytes 99848 | tf_op jit(solution)/shard_map/ppermute | solution.py:106
  412.4 4.0 collective-permute-start.9
  442.7 23.5 %collective-permute-start.14 = (bf16[512,1024]{0,1:T(8,128)(2,1)S(1)}, bf16[512,1024]{0,1:T(8,128)(2,1)}, u32[]{:S(2)}, u32[]{:S(2)}) collective-permute-start(bf16[512,1024]{0,1:T(8,128)(2,1)S(1)} %pad_maximum_fusion), channel_id=1, source_target_pairs={{0,2},{1,3},{2,0},{3,1},{4,6},{5,7},{6,4},{7,5},{8,10},{9,11},{10,... | collective-permute-start | bytes 3145736 | tf_op jit(solution)/shard_map/ppermute | solution.py:168
  444.4 47.6 %collective-permute-start.13 = (bf16[512,1024]{0,1:T(8,128)(2,1)S(1)}, bf16[512,1024]{0,1:T(8,128)(2,1)}, u32[]{:S(2)}, u32[]{:S(2)}) collective-permute-start(bf16[512,1024]{0,1:T(8,128)(2,1)S(1)} %pad_maximum_fusion), channel_id=1, source_target_pairs={{0,1},{1,2},{2,3},{3,0},{4,5},{5,6},{6,7},{7,4},{8,9},{9,10},{10,1... | collective-permute-start | bytes 3145736 | tf_op jit(solution)/shard_map/ppermute | solution.py:168
  446.4 50.5 %collective-permute-start.15 = (bf16[512,1024]{0,1:T(8,128)(2,1)S(1)}, bf16[512,1024]{0,1:T(8,128)(2,1)S(1)}, u32[]{:S(2)}, u32[]{:S(2)}) collective-permute-start(bf16[512,1024]{0,1:T(8,128)(2,1)S(1)} %pad_maximum_fusion), channel_id=1, source_target_pairs={{0,3},{1,0},{2,1},{3,2},{4,7},{5,4},{6,5},{7,6},{8,11},{9,8},{10,9... | collective-permute-start | bytes 3145736 | tf_op jit(solution)/shard_map/ppermute | solution.py:168
  (17 other events, 52.8 us)
